TPU v7x, 32 devices: a whole 2x2x4 slice. The times are simulated.
32 devices in a mesh: grp: 2 (over y), ctx: 8 (over z, x), pair: 2 (over core).
Axes of the slice: x: 2, y: 2, z: 4, core: 2. Of those that a mesh axis runs over, the one named last changes fastest.
Arguments:
- normed_input: bfloat16 [4, 1024, 2688], P(('grp', 'pair'), 'ctx'), parts along dimension 0, may hold values from -6 to 6
- queries: bfloat16 [4, 1024, 2048], P(('grp', 'pair'), 'ctx'), parts along dimension 0, may hold values from -64 to 64
- keys: bfloat16 [4, 1024, 1024], P(('grp', 'pair'), 'ctx'), parts along dimension 0, may hold values from -64 to 64
- value_projection: bfloat16 [2688, 1024], P('ctx'), may hold values from -0.125 to 0.125
- adapter_down: bfloat16 [2688, 16], replicated, may hold values from -0.125 to 0.125
- adapter_up: bfloat16 [16, 1024], replicated, may hold values from -1.5 to 1.5
- output_gradient: bfloat16 [4, 1024, 2048], P(('grp', 'pair'), 'ctx'), parts along dimension 0, may hold values from -6 to 6
- policy_logprob: float32 [4, 1024], P(('grp', 'pair'), 'ctx'), parts along dimension 0, may hold values from -6 to 0
- reference_logprob: float32 [4, 1024], P(('grp', 'pair'), 'ctx'), parts along dimension 0, may hold values from -8 to 0
- token_pair_index: int32 [4, 1024], P(('grp', 'pair'), 'ctx'), parts along dimension 0, may hold values from 0 to 7, never falling along the last dimension, each value on 1 to 1017 neighbouring positions
Outputs:
- input_grad: bfloat16 [4, 1024, 2688], P(('grp', 'pair'), 'ctx'), parts along dimension 0
- query_grad: bfloat16 [4, 1024, 2048], P(('grp', 'pair'), 'ctx'), parts along dimension 0
- key_grad: bfloat16 [4, 1024, 1024], P(('grp', 'pair'), 'ctx'), parts along dimension 0
- down_gradient: float32 [5376, 16], P('grp'), parts along dimension 0
- up_gradient: float32 [32, 1024], P('grp'), parts along dimension 0
There are 2 independent parts, one for each index of `grp`. A program takes and returns all parts, laid end to end along the dimension named above; an argument that names none is the same for every part. Nothing has to cross between parts.
Inputs may be any that keep to these rules, and one draw needn't show every extreme that they name: `token_pair_index`: along each sequence the ids never fall; both sequences hold every id, each segment at most 1017 tokens and one exactly 1017.
All inputs are finite; a program needn't handle non-finite values.
Results may differ from a plain program's by a relative error of at most 0.03.
Values may be sent and summed in bfloat16 or wider, within the bound.
No kernel may reach another device: no remote copies, remote signals or barrier semaphores. Data moves between devices by JAX's collectives and lax.ppermute only.
A program may use at most 128 MiB of HBM per device.

v0:
```python
import jax
import jax.numpy as jnp
from jax import lax
from jax.sharding import PartitionSpec as P

HEAD_SIZE = 128
WINDOW = 1024
SEGS = 8
DPO_BETA = 0.1
LOSS_SCALE = 256.0
ADAPTER_SCALE = 2.0
ATTN_SCALE = 168.0 ** (-0.5)
NEG_FILL = -1e30


def from_partner(shard, axis, stride):
    return lax.ppermute(shard, axis, [(i, i ^ 1 << stride) for i in range(lax.axis_size(axis))])


def shifted(block, axis, distance):
    devices = range(lax.axis_size(axis))
    route = [(i - distance, i) for i in devices if i - distance in devices]
    return lax.ppermute(block, axis, route)


def shards(
    normed_input,
    queries,
    keys,
    value_projection,
    adapter_down,
    adapter_up,
    output_gradient,
    policy_logprob,
    reference_logprob,
    token_pair_index,
):
    tok_rows = normed_input.shape[1]
    width_kv = keys.shape[2]
    kv_heads = width_kv // HEAD_SIZE
    group_size = queries.shape[2] // width_kv
    hidden_rows = normed_input[0]
    own_keys = keys[0]
    pair_index = lax.axis_index("pair")
    ctx_index = lax.axis_index("ctx")
    half_cols = width_kv // 2
    own_half = lax.dynamic_slice_in_dim(value_projection, pair_index * half_cols, half_cols, 1)
    rows_half = lax.all_gather(own_half, "ctx", axis=0, tiled=True)
    full_weight = lax.all_gather(rows_half, "pair", axis=1, tiled=True)
    rank_projection = jnp.dot(hidden_rows, adapter_down, preferred_element_type=jnp.float32).astype(
        jnp.bfloat16
    )
    values = (
        jnp.dot(hidden_rows, full_weight, preferred_element_type=jnp.float32)
        + ADAPTER_SCALE * jnp.dot(rank_projection, adapter_up, preferred_element_type=jnp.float32)
    ).astype(jnp.bfloat16)
    segment_labels = token_pair_index[0]
    seg_table = (segment_labels[:, None] == jnp.arange(SEGS, dtype=jnp.int32)[None, :]).astype(
        jnp.float32
    )
    log_gap = policy_logprob[0] - reference_logprob[0]
    part_diff = jnp.sum(seg_table * log_gap[:, None], 0)
    part_count = jnp.sum(seg_table, 0)
    own_diff, counts = lax.psum((part_diff, part_count), "ctx")
    other_diff = from_partner(own_diff, "pair", 0)
    direction = 1.0 - 2.0 * pair_index.astype(jnp.float32)
    margin = DPO_BETA * (direction * (own_diff - other_diff))
    coef = -direction * DPO_BETA * LOSS_SCALE * jax.nn.sigmoid(-margin)
    starts = jnp.cumsum(counts) - counts
    tok_start = jnp.sum(seg_table * starts[None, :], 1).astype(jnp.int32)
    token_coefficient = jnp.sum(seg_table * coef[None, :], 1)
    halo_blocks = min(WINDOW // tok_rows, lax.axis_size("ctx") - 1)
    key_blocks = []
    value_blocks = []
    for distance in range(halo_blocks, 0, -1):
        key_blocks.append(shifted(own_keys, "ctx", distance))
        value_blocks.append(shifted(values, "ctx", distance))
    all_keys = jnp.concatenate(key_blocks + [own_keys], 0)
    all_keys, own_values = lax.optimization_barrier((all_keys, values))
    all_values = jnp.concatenate(value_blocks + [own_values], 0)
    span = all_keys.shape[0]
    tpos = ctx_index * tok_rows + jnp.arange(tok_rows, dtype=jnp.int32)
    upos = ctx_index * tok_rows - halo_blocks * tok_rows + jnp.arange(span, dtype=jnp.int32)
    allowed = (
        (upos[None, :] <= tpos[:, None])
        & (upos[None, :] > tpos[:, None] - WINDOW)
        & (upos[None, :] >= tok_start[:, None])
    )
    coef_rows = token_coefficient[None, :, None]
    query_rows = queries[0].reshape(tok_rows, kv_heads, group_size, HEAD_SIZE)
    grad_rows = output_gradient[0].reshape(tok_rows, kv_heads, group_size, HEAD_SIZE)
    key_rows = all_keys.reshape(span, kv_heads, HEAD_SIZE)
    value_rows = all_values.reshape(span, kv_heads, HEAD_SIZE)
    scores = ATTN_SCALE * jnp.einsum(
        "tjgd,ljd->jgtl", query_rows, key_rows, preferred_element_type=jnp.float32
    )
    masked = jnp.where(allowed[None, None], scores, NEG_FILL)
    row_max = jnp.max(masked, -1, keepdims=True)
    weights_exp = jnp.where(allowed[None, None], jnp.exp(masked - row_max), 0.0)
    attn_probs = weights_exp / jnp.sum(weights_exp, -1, keepdims=True)
    prob_grad = coef_rows[None] * jnp.einsum(
        "tjgd,ljd->jgtl", grad_rows, value_rows, preferred_element_type=jnp.float32
    )
    row_delta = jnp.sum(attn_probs * prob_grad, -1, keepdims=True)
    score_grad = (ATTN_SCALE * attn_probs * (prob_grad - row_delta)).astype(jnp.bfloat16)
    query_grad = (
        jnp.einsum("jgtl,ljd->tjgd", score_grad, key_rows, preferred_element_type=jnp.float32)
        .astype(jnp.bfloat16)
        .reshape(tok_rows, kv_heads * group_size * HEAD_SIZE)
    )
    key_parts = jnp.einsum(
        "jgtl,tjgd->ljd", score_grad, query_rows, preferred_element_type=jnp.float32
    ).reshape(span, width_kv)
    weighted = (attn_probs * coef_rows[None]).astype(jnp.bfloat16)
    value_parts = jnp.einsum(
        "jgtl,tjgd->ljd", weighted, grad_rows, preferred_element_type=jnp.float32
    ).reshape(span, width_kv)
    key_total = key_parts[halo_blocks * tok_rows :]
    value_total = value_parts[halo_blocks * tok_rows :]
    for distance in range(1, halo_blocks + 1):
        block_start = (halo_blocks - distance) * tok_rows
        send_keys = key_parts[block_start : block_start + tok_rows].astype(jnp.bfloat16)
        send_values = value_parts[block_start : block_start + tok_rows].astype(jnp.bfloat16)
        back_keys, back_values = shifted((send_keys, send_values), "ctx", -distance)
        key_total = key_total + back_keys.astype(jnp.float32)
        value_total = value_total + back_values.astype(jnp.float32)
    key_grad = key_total.astype(jnp.bfloat16)
    value_gradient = value_total.astype(jnp.bfloat16)
    rank_middle = jnp.einsum(
        "sj,zj->sz", value_gradient, adapter_up, preferred_element_type=jnp.float32
    ).astype(jnp.bfloat16)
    input_grad = (
        jnp.einsum("tk,dk->td", value_gradient, full_weight, preferred_element_type=jnp.float32)
        + ADAPTER_SCALE
        * jnp.einsum("pb,wb->pw", rank_middle, adapter_down, preferred_element_type=jnp.float32)
    ).astype(jnp.bfloat16)
    up_factor = ADAPTER_SCALE * jnp.einsum(
        "tr,tk->rk", rank_projection, value_gradient, preferred_element_type=jnp.float32
    )
    down_factor = ADAPTER_SCALE * jnp.einsum(
        "td,tr->dr", hidden_rows, rank_middle, preferred_element_type=jnp.float32
    )
    down_gradient, up_gradient = lax.psum((down_factor, up_factor), ("ctx", "pair"))
    return (input_grad[None], query_grad[None], key_grad[None], down_gradient, up_gradient)


def solution(mesh):
    return jax.shard_map(
        shards,
        mesh=mesh,
        in_specs=(
            P(("grp", "pair"), "ctx", None),
            P(("grp", "pair"), "ctx", None),
            P(("grp", "pair"), "ctx", None),
            P("ctx", None),
            P(),
            P(),
            P(("grp", "pair"), "ctx", None),
            P(("grp", "pair"), "ctx"),
            P(("grp", "pair"), "ctx"),
            P(("grp", "pair"), "ctx"),
        ),
        out_specs=(
            P(("grp", "pair"), "ctx", None),
            P(("grp", "pair"), "ctx", None),
            P(("grp", "pair"), "ctx", None),
            P("grp", None),
            P("grp", None),
        ),
        check_vma=False,
    )
```

profile of v0, /device:TPU:8, one launch (start us, length us, event | category | flops | bytes accessed | tf_op | source)
XLA Modules:
  0.0 361.4 jit_solution(16586474015925666652)
XLA Ops:
  9.2 58.9 %all-gather.3.cloned.1.call-done = bf16[2688,512]{1,0:T(8,128)(2,1)} async-done(((bf16[336,512]{1,0:T(8,128)(2,1)}), bf16[2688,512]{1,0:T(8,128)(2,1)}) %all-gather.3.cloned.1.call-update) | async-done | bytes 2752528 | tf_op jit(solution)/shard_map/all_gather | solution.py:48
  70.2 4.2 %collective-permute-start.2 = (bf16[128,1024]{1,0:T(8,128)(2,1)}, bf16[128,1024]{1,0:T(8,128)(2,1)}, u32[]{:S(2)}, u32[]{:S(2)}) collective-permute-start(bf16[128,1024]{1,0:T(8,128)(2,1)} %bitcast.3), channel_id=1, source_target_pairs={{0,10},{2,12},{4,14},{1,11},{3,13},{5,15},{16,26},{18,28},{20,30},... | collective-permute-start | bytes 786440 | tf_op jit(solution)/shard_map/ppermute | solution.py:23
  74.3 2.0 collective-permute-start.3
  76.5 30.3 %all-reduce.1 = (f32[8]{0:T(128)S(1)}, f32[8]{0:T(128)S(1)}) all-reduce(f32[8]{0:T(128)S(1)} %get-tuple-element.21, f32[8]{0:T(128)S(1)} %get-tuple-element.22), channel_id=1, replica_groups=mesh['grp'=2,'ctx'=8,'pair'=2] {'ctx'}, use_global_device_ids=true, to_apply=%region_1.0 | all-reduce | flops 16 | bytes 128 | tf_op jit(solution)/shard_map/psum | solution.py:64
  108.8 2.9 collective-permute-start.4
  113.4 3.2 collective-permute-start.5
  117.5 1.9 collective-permute-start.6
  122.4 3.8 %collective-permute-done.5 = bf16[128,1024]{1,0:T(8,128)(2,1)S(1)} collective-permute-done((bf16[128,1024]{1,0:T(8,128)(2,1)}, bf16[128,1024]{1,0:T(8,128)(2,1)S(1)}, u32[]{:S(2)}, u32[]{:S(2)}) %collective-permute-start.5) | collective-permute-done | bytes 262176 | tf_op jit(solution)/shard_map/ppermute | solution.py:23
  126.3 4.2 %collective-permute-done.6 = bf16[128,1024]{1,0:T(8,128)(2,1)S(1)} collective-permute-done((bf16[128,1024]{1,0:T(8,128)(2,1)}, bf16[128,1024]{1,0:T(8,128)(2,1)S(1)}, u32[]{:S(2)}, u32[]{:S(2)}) %collective-permute-start.6) | collective-permute-done | bytes 262176 | tf_op jit(solution)/shard_map/ppermute | solution.py:23
  131.5 4.2 %convolution_bitcast_fusion.1 = f32[128,1024]{0,1:T(8,128)S(1)} fusion(bf16[2688,1024]{1,0:T(8,128)(2,1)} %all-gather.5.cloned.1.call-done, bf16[1,128,2688]{2,1,0:T(8,128)(2,1)S(1)} %copy-done), kind=kOutput, calls=%fused_computation.26 | convolution fusion | flops 704643072 | bytes 6717440 | tf_op jit(solution)/shard_map/dot_general | solution.py:54
  139.4 2.3 collective-permute-start.17
  141.6 6.5 %collective-permute-start.18 = (bf16[128,1024]{0,1:T(8,128)(2,1)}, bf16[128,1024]{0,1:T(8,128)(2,1)}, u32[]{:S(2)}, u32[]{:S(2)}) collective-permute-start(bf16[128,1024]{0,1:T(8,128)(2,1)} %fusion.15), channel_id=1, source_target_pairs={{0,8},{2,10},{4,12},{6,14},{1,9},{3,11},{5,13},{7,15},{16,24},{18,... | collective-permute-start | bytes 786440 | tf_op jit(solution)/shard_map/ppermute | solution.py:23
  148.2 2.0 collective-permute-start.19
  150.2 2.0 copy.71
  152.1 3.2 copy.60
  155.4 6.9 %fusion.36 = (f32[8,2,128]{2,1,0:T(2,128)S(1)}, f32[8,2,128,1024]{2,3,1,0:T(8,128)}) fusion(pred[128,1024]{0,1:T(8,128)(4,1)} %compare_and_fusion, bf16[1024,8,128,1]{0,2,3,1:T(8,128)(2,1)S(1)} %copy.60, bf16[128,8,2,128]{0,3,2,1:T(8,128)(2,1)S(1)} %bitcast.126), kind=kOutput, calls=%fused_computation.82 | convolution fusion | flops 547357696 | bytes 11149312 | tf_op jit(solution)/shard_map/sub | solution.py:99
  162.3 5.1 %fusion.37 = (bf16[1024,8,128]{0,2,1:T(8,128)(2,1)S(1)}, f32[1024,8,128]{0,2,1:T(8,128)S(1)}) fusion(bf16[128,8,2,128]{3,2,1,0:T(2,128)(2,1)} %reshape_squeeze.7, f32[128]{0:T(128)S(1)} %get-tuple-element.20, f32[8,2,128,1024]{2,3,1,0:T(8,128)} %get-tuple-element.42, f32[8,2,128]{2,1,0:T(2,128)S(1)} %get-tuple-element.41), kind=kOutput, calls=%fused_computation.83 | convolution fusion | flops 544210944 | bytes 15213056 | tf_op jit(solution)/shard_map/jgtl,tjgd->ljd/dot_general | solution.py:115
  168.0 2.9 collective-permute-start.20
  172.0 1.9 collective-permute-start.21
  180.8 3.2 collective-permute-done.20
  188.1 1.9 fusion.1
  193.4 2.9 collective-permute-start.9
  196.3 3.1 collective-permute-start.8
  199.5 3.5 fusion.38
  203.1 19.5 %collective-permute-done.10 = bf16[128,1024]{0,1:T(8,128)(2,1)S(1)} collective-permute-done((bf16[128,1024]{0,1:T(8,128)(2,1)S(1)}, bf16[128,1024]{0,1:T(8,128)(2,1)S(1)}, u32[]{:S(2)}, u32[]{:S(2)}) %collective-permute-start.10) | collective-permute-done | bytes 262176 | tf_op jit(solution)/shard_map/ppermute | solution.py:23
  225.4 2.0 copy.54
  245.5 1.9 collective-permute-start.23
  249.4 5.3 %fusion.11 = bf16[1,128,2688]{2,1,0:T(8,128)(2,1)} fusion(f32[128,2688]{1,0:T(8,128)S(1)} %convolution_multiply_fusion, bf16[128,1024]{0,1:T(8,128)(2,1)S(1)} %fusion.27, bf16[2688,1024]{1,0:T(8,128)(2,1)} %all-gather.5.cloned.1.call-done), kind=kOutput, calls=%fused_computation.19 | convolution fusion | flops 705331200 | bytes 7831552 | tf_op jit(solution)/shard_map/tk,dk->td/dot_general | solution.py:133
  254.7 16.3 %collective-permute-done.24 = bf16[128,1024]{1,0:T(8,128)(2,1)} collective-permute-done((bf16[128,1024]{1,0:T(8,128)(2,1)}, bf16[128,1024]{1,0:T(8,128)(2,1)}, u32[]{:S(2)}, u32[]{:S(2)}) %collective-permute-start.24) | collective-permute-done | bytes 262176 | tf_op jit(solution)/shard_map/ppermute | solution.py:23
  271.1 3.9 %collective-permute-done.23 = bf16[128,1024]{1,0:T(8,128)(2,1)S(1)} collective-permute-done((bf16[128,1024]{1,0:T(8,128)(2,1)}, bf16[128,1024]{1,0:T(8,128)(2,1)S(1)}, u32[]{:S(2)}, u32[]{:S(2)}) %collective-permute-start.23) | collective-permute-done | bytes 262176 | tf_op jit(solution)/shard_map/ppermute | solution.py:23
  275.0 2.0 fusion.31
  277.0 74.8 %all-reduce.4.cloned.1.call-done = (f32[2688,16]{0,1:T(8,128)}, f32[16,1024]{1,0:T(8,128)}) async-done(((f32[2688,16]{0,1:T(8,128)}, f32[16,1024]{1,0:T(8,128)}), (f32[2688,16]{0,1:T(8,128)}, f32[16,1024]{1,0:T(8,128)})) %all-reduce.4.cloned.1.call-update) | async-done | bytes 237584 | tf_op jit(solution)/shard_map/psum | solution.py:143
  (129 shorter events, 58.2 us)
Async XLA Ops:
  7.2 60.8 %all-gather.3.cloned.1.call-start = ((), (), s32[]{:S(2)}) async-start(), calls=%async_computation | async-start | bytes 3096576 | tf_op jit(solution)/shard_map/all_gather | solution.py:48
  9.1 122.3 %all-gather.5.cloned.1.call-start = ((), (), s32[]{:S(2)}) async-start(), calls=%async_computation.1 | async-start | bytes 8257536 | tf_op jit(solution)/shard_map/all_gather | solution.py:49
  68.1 283.8 %all-reduce.4.cloned.1.call-start = ((), (), s32[]{:S(2)}) async-start(), calls=%async_computation.2 | async-start | bytes 475136 | tf_op jit(solution)/shard_map/psum | solution.py:143
  68.1 44.5 %collective-permute-start = (bf16[128,1024]{1,0:T(8,128)(2,1)}, bf16[128,1024]{1,0:T(8,128)(2,1)S(1)}, u32[]{:S(2)}, u32[]{:S(2)}) collective-permute-start(bf16[128,1024]{1,0:T(8,128)(2,1)} %bitcast.3), channel_id=1, source_target_pairs={{0,14},{1,15},{16,30},{17,31}} | collective-permute-start | bytes 786440 | tf_op jit(solution)/shard_map/ppermute | solution.py:23
  68.8 48.7 %collective-permute-start.1 = (bf16[128,1024]{1,0:T(8,128)(2,1)}, bf16[128,1024]{1,0:T(8,128)(2,1)}, u32[]{:S(2)}, u32[]{:S(2)}) collective-permute-start(bf16[128,1024]{1,0:T(8,128)(2,1)} %bitcast.3), channel_id=1, source_target_pairs={{0,12},{2,14},{1,13},{3,15},{16,28},{18,30},{17,29},{19,31}} | collective-permute-start | bytes 786440 | tf_op jit(solution)/shard_map/ppermute | solution.py:23
  70.2 50.3 %collective-permute-start.2 = (bf16[128,1024]{1,0:T(8,128)(2,1)}, bf16[128,1024]{1,0:T(8,128)(2,1)}, u32[]{:S(2)}, u32[]{:S(2)}) collective-permute-start(bf16[128,1024]{1,0:T(8,128)(2,1)} %bitcast.3), channel_id=1, source_target_pairs={{0,10},{2,12},{4,14},{1,11},{3,13},{5,15},{16,26},{18,28},{20,30},... | collective-permute-start | bytes 786440 | tf_op jit(solution)/shard_map/ppermute | solution.py:23
  74.3 47.1 %collective-permute-start.3 = (bf16[128,1024]{1,0:T(8,128)(2,1)}, bf16[128,1024]{1,0:T(8,128)(2,1)}, u32[]{:S(2)}, u32[]{:S(2)}) collective-permute-start(bf16[128,1024]{1,0:T(8,128)(2,1)} %bitcast.3), channel_id=1, source_target_pairs={{0,8},{2,10},{4,12},{6,14},{1,9},{3,11},{5,13},{7,15},{16,24},{18,... | collective-permute-start | bytes 786440 | tf_op jit(solution)/shard_map/ppermute | solution.py:23
  106.8 2.0 collective-permute-start.7
  108.8 13.6 %collective-permute-start.4 = (bf16[128,1024]{1,0:T(8,128)(2,1)}, bf16[128,1024]{1,0:T(8,128)(2,1)S(1)}, u32[]{:S(2)}, u32[]{:S(2)}) collective-permute-start(bf16[128,1024]{1,0:T(8,128)(2,1)} %bitcast.3), channel_id=1, source_target_pairs={{0,6},{2,8},{4,10},{6,12},{8,14},{1,7},{3,9},{5,11},{7,13},{9,15},... | collective-permute-start | bytes 786440 | tf_op jit(solution)/shard_map/ppermute | solution.py:23
  113.4 12.9 %collective-permute-start.5 = (bf16[128,1024]{1,0:T(8,128)(2,1)}, bf16[128,1024]{1,0:T(8,128)(2,1)S(1)}, u32[]{:S(2)}, u32[]{:S(2)}) collective-permute-start(bf16[128,1024]{1,0:T(8,128)(2,1)} %bitcast.3), channel_id=1, source_target_pairs={{0,4},{2,6},{4,8},{6,10},{8,12},{10,14},{1,5},{3,7},{5,9},{7,11},{... | collective-permute-start | bytes 786440 | tf_op jit(solution)/shard_map/ppermute | solution.py:23
  117.5 12.9 %collective-permute-start.6 = (bf16[128,1024]{1,0:T(8,128)(2,1)}, bf16[128,1024]{1,0:T(8,128)(2,1)S(1)}, u32[]{:S(2)}, u32[]{:S(2)}) collective-permute-start(bf16[128,1024]{1,0:T(8,128)(2,1)} %bitcast.3), channel_id=1, source_target_pairs={{0,2},{2,4},{4,6},{6,8},{8,10},{10,12},{12,14},{1,3},{3,5},{5,7},{... | collective-permute-start | bytes 786440 | tf_op jit(solution)/shard_map/ppermute | solution.py:23
  136.7 31.4 %collective-permute-start.15 = (bf16[128,1024]{0,1:T(8,128)(2,1)}, bf16[128,1024]{0,1:T(8,128)(2,1)}, u32[]{:S(2)}, u32[]{:S(2)}) collective-permute-start(bf16[128,1024]{0,1:T(8,128)(2,1)} %fusion.15), channel_id=1, source_target_pairs={{0,14},{1,15},{16,30},{17,31}} | collective-permute-start | bytes 786440 | tf_op jit(solution)/shard_map/ppermute | solution.py:23
  138.0 34.0 %collective-permute-start.16 = (bf16[128,1024]{0,1:T(8,128)(2,1)}, bf16[128,1024]{0,1:T(8,128)(2,1)}, u32[]{:S(2)}, u32[]{:S(2)}) collective-permute-start(bf16[128,1024]{0,1:T(8,128)(2,1)} %fusion.15), channel_id=1, source_target_pairs={{0,12},{2,14},{1,13},{3,15},{16,28},{18,30},{17,29},{19,31}} | collective-permute-start | bytes 786440 | tf_op jit(solution)/shard_map/ppermute | solution.py:23
  139.4 35.6 %collective-permute-start.17 = (bf16[128,1024]{0,1:T(8,128)(2,1)}, bf16[128,1024]{0,1:T(8,128)(2,1)}, u32[]{:S(2)}, u32[]{:S(2)}) collective-permute-start(bf16[128,1024]{0,1:T(8,128)(2,1)} %fusion.15), channel_id=1, source_target_pairs={{0,10},{2,12},{4,14},{1,11},{3,13},{5,15},{16,26},{18,28},{20,30},... | collective-permute-start | bytes 786440 | tf_op jit(solution)/shard_map/ppermute | solution.py:23
  141.6 35.1 %collective-permute-start.18 = (bf16[128,1024]{0,1:T(8,128)(2,1)}, bf16[128,1024]{0,1:T(8,128)(2,1)}, u32[]{:S(2)}, u32[]{:S(2)}) collective-permute-start(bf16[128,1024]{0,1:T(8,128)(2,1)} %fusion.15), channel_id=1, source_target_pairs={{0,8},{2,10},{4,12},{6,14},{1,9},{3,11},{5,13},{7,15},{16,24},{18,... | collective-permute-start | bytes 786440 | tf_op jit(solution)/shard_map/ppermute | solution.py:23
  148.2 30.3 %collective-permute-start.19 = (bf16[128,1024]{0,1:T(8,128)(2,1)}, bf16[128,1024]{0,1:T(8,128)(2,1)}, u32[]{:S(2)}, u32[]{:S(2)}) collective-permute-start(bf16[128,1024]{0,1:T(8,128)(2,1)} %fusion.15), channel_id=1, source_target_pairs={{0,6},{2,8},{4,10},{6,12},{8,14},{1,7},{3,9},{5,11},{7,13},{9,15},... | collective-permute-start | bytes 786440 | tf_op jit(solution)/shard_map/ppermute | solution.py:23
  168.0 15.9 %collective-permute-start.20 = (bf16[128,1024]{0,1:T(8,128)(2,1)}, bf16[128,1024]{0,1:T(8,128)(2,1)S(1)}, u32[]{:S(2)}, u32[]{:S(2)}) collective-permute-start(bf16[128,1024]{0,1:T(8,128)(2,1)} %fusion.15), channel_id=1, source_target_pairs={{0,4},{2,6},{4,8},{6,10},{8,12},{10,14},{1,5},{3,7},{5,9},{7,11},{... | collective-permute-start | bytes 786440 | tf_op jit(solution)/shard_map/ppermute | solution.py:23
  172.0 13.5 %collective-permute-start.21 = (bf16[128,1024]{0,1:T(8,128)(2,1)}, bf16[128,1024]{0,1:T(8,128)(2,1)S(1)}, u32[]{:S(2)}, u32[]{:S(2)}) collective-permute-start(bf16[128,1024]{0,1:T(8,128)(2,1)} %fusion.15), channel_id=1, source_target_pairs={{0,2},{2,4},{4,6},{6,8},{8,10},{10,12},{12,14},{1,3},{3,5},{5,7},{... | collective-permute-start | bytes 786440 | tf_op jit(solution)/shard_map/ppermute | solution.py:23
  175.0 18.5 %collective-permute-start.14 = (bf16[128,1024]{0,1:T(8,128)(2,1)S(1)}, bf16[128,1024]{0,1:T(8,128)(2,1)S(1)}, u32[]{:S(2)}, u32[]{:S(2)}) collective-permute-start(bf16[128,1024]{0,1:T(8,128)(2,1)S(1)} %bitcast.141), channel_id=1, source_target_pairs={{14,0},{15,1},{30,16},{31,17}} | collective-permute-start | bytes 786440 | tf_op jit(solution)/shard_map/ppermute | solution.py:23
  176.7 19.6 %collective-permute-start.13 = (bf16[128,1024]{0,1:T(8,128)(2,1)S(1)}, bf16[128,1024]{0,1:T(8,128)(2,1)S(1)}, u32[]{:S(2)}, u32[]{:S(2)}) collective-permute-start(bf16[128,1024]{0,1:T(8,128)(2,1)S(1)} %bitcast.140), channel_id=1, source_target_pairs={{12,0},{14,2},{13,1},{15,3},{28,16},{30,18},{29,17},{31,19}} | collective-permute-start | bytes 786440 | tf_op jit(solution)/shard_map/ppermute | solution.py:23
  178.4 24.5 %collective-permute-start.12 = (bf16[128,1024]{0,1:T(8,128)(2,1)S(1)}, bf16[128,1024]{0,1:T(8,128)(2,1)S(1)}, u32[]{:S(2)}, u32[]{:S(2)}) collective-permute-start(bf16[128,1024]{0,1:T(8,128)(2,1)S(1)} %bitcast.139), channel_id=1, source_target_pairs={{10,0},{12,2},{14,4},{11,1},{13,3},{15,5},{26,16},{28,18},{30,20},... | collective-permute-start | bytes 786440 | tf_op jit(solution)/shard_map/ppermute | solution.py:23
  184.0 19.2 %collective-permute-start.11 = (bf16[128,1024]{0,1:T(8,128)(2,1)S(1)}, bf16[128,1024]{0,1:T(8,128)(2,1)S(1)}, u32[]{:S(2)}, u32[]{:S(2)}) collective-permute-start(bf16[128,1024]{0,1:T(8,128)(2,1)S(1)} %bitcast.138), channel_id=1, source_target_pairs={{8,0},{10,2},{12,4},{14,6},{9,1},{11,3},{13,5},{15,7},{24,16},{26,... | collective-permute-start | bytes 786440 | tf_op jit(solution)/shard_map/ppermute | solution.py:23
  185.5 37.2 %collective-permute-start.10 = (bf16[128,1024]{0,1:T(8,128)(2,1)S(1)}, bf16[128,1024]{0,1:T(8,128)(2,1)S(1)}, u32[]{:S(2)}, u32[]{:S(2)}) collective-permute-start(bf16[128,1024]{0,1:T(8,128)(2,1)S(1)} %bitcast.137), channel_id=1, source_target_pairs={{6,0},{8,2},{10,4},{12,6},{14,8},{7,1},{9,3},{11,5},{13,7},{15,9},... | collective-permute-start | bytes 786440 | tf_op jit(solution)/shard_map/ppermute | solution.py:23
  193.4 30.7 %collective-permute-start.9 = (bf16[128,1024]{0,1:T(8,128)(2,1)S(1)}, bf16[128,1024]{0,1:T(8,128)(2,1)S(1)}, u32[]{:S(2)}, u32[]{:S(2)}) collective-permute-start(bf16[128,1024]{0,1:T(8,128)(2,1)S(1)} %bitcast.136), channel_id=1, source_target_pairs={{4,0},{6,2},{8,4},{10,6},{12,8},{14,10},{5,1},{7,3},{9,5},{11,7},{... | collective-permute-start | bytes 786440 | tf_op jit(solution)/shard_map/ppermute | solution.py:23
  196.3 27.8 %collective-permute-start.8 = (bf16[128,1024]{0,1:T(8,128)(2,1)S(1)}, bf16[128,1024]{0,1:T(8,128)(2,1)S(1)}, u32[]{:S(2)}, u32[]{:S(2)}) collective-permute-start(bf16[128,1024]{0,1:T(8,128)(2,1)S(1)} %bitcast.135), channel_id=1, source_target_pairs={{2,0},{4,2},{6,4},{8,6},{10,8},{12,10},{14,12},{3,1},{5,3},{7,5},{... | collective-permute-start | bytes 786440 | tf_op jit(solution)/shard_map/ppermute | solution.py:23
  230.7 14.8 %collective-permute-start.28 = (bf16[128,1024]{1,0:T(8,128)(2,1)}, bf16[128,1024]{1,0:T(8,128)(2,1)S(1)}, u32[]{:S(2)}, u32[]{:S(2)}) collective-permute-start(bf16[128,1024]{1,0:T(8,128)(2,1)} %copy.53), channel_id=1, source_target_pairs={{14,0},{15,1},{30,16},{31,17}} | collective-permute-start | bytes 786440 | tf_op jit(solution)/shard_map/ppermute | solution.py:23
  233.2 14.2 %collective-permute-start.27 = (bf16[128,1024]{1,0:T(8,128)(2,1)}, bf16[128,1024]{1,0:T(8,128)(2,1)S(1)}, u32[]{:S(2)}, u32[]{:S(2)}) collective-permute-start(bf16[128,1024]{1,0:T(8,128)(2,1)} %copy.52), channel_id=1, source_target_pairs={{12,0},{14,2},{13,1},{15,3},{28,16},{30,18},{29,17},{31,19}} | collective-permute-start | bytes 786440 | tf_op jit(solution)/shard_map/ppermute | solution.py:23
  235.7 19.1 %collective-permute-start.26 = (bf16[128,1024]{1,0:T(8,128)(2,1)}, bf16[128,1024]{1,0:T(8,128)(2,1)S(1)}, u32[]{:S(2)}, u32[]{:S(2)}) collective-permute-start(bf16[128,1024]{1,0:T(8,128)(2,1)} %copy.51), channel_id=1, source_target_pairs={{10,0},{12,2},{14,4},{11,1},{13,3},{15,5},{26,16},{28,18},{30,20},... | collective-permute-start | bytes 786440 | tf_op jit(solution)/shard_map/ppermute | solution.py:23
  238.7 16.0 %collective-permute-start.25 = (bf16[128,1024]{1,0:T(8,128)(2,1)}, bf16[128,1024]{1,0:T(8,128)(2,1)S(1)}, u32[]{:S(2)}, u32[]{:S(2)}) collective-permute-start(bf16[128,1024]{1,0:T(8,128)(2,1)} %copy.50), channel_id=1, source_target_pairs={{8,0},{10,2},{12,4},{14,6},{9,1},{11,3},{13,5},{15,7},{24,16},{26,... | collective-permute-start | bytes 786440 | tf_op jit(solution)/shard_map/ppermute | solution.py:23
  240.8 30.2 %collective-permute-start.24 = (bf16[128,1024]{1,0:T(8,128)(2,1)}, bf16[128,1024]{1,0:T(8,128)(2,1)}, u32[]{:S(2)}, u32[]{:S(2)}) collective-permute-start(bf16[128,1024]{1,0:T(8,128)(2,1)} %copy.49), channel_id=1, source_target_pairs={{6,0},{8,2},{10,4},{12,6},{14,8},{7,1},{9,3},{11,5},{13,7},{15,9},... | collective-permute-start | bytes 786440 | tf_op jit(solution)/shard_map/ppermute | solution.py:23
  245.5 29.5 %collective-permute-start.23 = (bf16[128,1024]{1,0:T(8,128)(2,1)}, bf16[128,1024]{1,0:T(8,128)(2,1)S(1)}, u32[]{:S(2)}, u32[]{:S(2)}) collective-permute-start(bf16[128,1024]{1,0:T(8,128)(2,1)} %copy.48), channel_id=1, source_target_pairs={{4,0},{6,2},{8,4},{10,6},{12,8},{14,10},{5,1},{7,3},{9,5},{11,7},{... | collective-permute-start | bytes 786440 | tf_op jit(solution)/shard_map/ppermute | solution.py:23
  247.4 27.6 %collective-permute-start.22 = (bf16[128,1024]{1,0:T(8,128)(2,1)}, bf16[128,1024]{1,0:T(8,128)(2,1)S(1)}, u32[]{:S(2)}, u32[]{:S(2)}) collective-permute-start(bf16[128,1024]{1,0:T(8,128)(2,1)} %copy.46), channel_id=1, source_target_pairs={{2,0},{4,2},{6,4},{8,6},{10,8},{12,10},{14,12},{3,1},{5,3},{7,5},{... | collective-permute-start | bytes 786440 | tf_op jit(solution)/shard_map/ppermute | solution.py:23
  (15 other events, 657.8 us)
Sparse Core Ops, SparseCore 0:
  10.8 57.1 all-gather.2
  69.6 14.4 all-gather.4
  245.2 106.5 all-reduce.3
where the time goes:
time: 363 us; the launch traced here: 361 us
  waiting for transfers between devices  187 us (52%)
  starting transfers between devices  55.1 us (15%)
  local copies, waits for them, and re-layouts  37.7 us (10%)
  matrix products  32 us (9%)
  blocking collectives  30.3 us (8%)
  between operations  14.4 us (4%)
  other arithmetic  5.29 us (1%)
    psum x1, waiting for transfers between devices, shards(): lax.psum((down_factor, up_factor), ('ctx', 'pair'))  74.8 us
    all_gather x1, waiting for transfers between devices, shards(): rows_half = lax.all_gather(own_half, 'ctx', axis=0, tiled=True)  58.9 us
    ppermute x28, starting transfers between devices, shifted(): return lax.ppermute(block, axis, route)  55 us
    ppermute x28, waiting for transfers between devices, shifted(): return lax.ppermute(block, axis, route)  52.8 us
    psum x1, blocking collectives, shards(): own_diff, counts = lax.psum((part_diff, part_count), 'ctx')  30.3 us
    unnamed x48, local copies, waits for them, and re-layouts  17.1 us
    convert_element_type x7, local copies, waits for them, and re-layouts, shards(): key_parts[block_start:block_start + tok_rows].astype(jnp.bfloat16)  8.84 us
  transfers between devices with their start and end apart: 32, of which 11 were waited for; matrix products, arithmetic and copies ran while one was open for 16% of the time, Pallas kernels for 0%

commit v1 on v0

--- a/solution.py
+++ b/solution.py
@@ -45,7 +45,12 @@
     ctx_index = lax.axis_index("ctx")
     half_cols = width_kv // 2
     own_half = lax.dynamic_slice_in_dim(value_projection, pair_index * half_cols, half_cols, 1)
-    rows_half = lax.all_gather(own_half, "ctx", axis=0, tiled=True)
+    ring = [own_half]
+    for hop in range(7):
+        ring.append(lax.ppermute(ring[-1], "ctx", [(dev, (dev + 1) % 8) for dev in range(8)]))
+    rows_half = jnp.roll(
+        jnp.concatenate(ring[::-1], axis=0), (lax.axis_index("ctx") + 1) * ring[0].shape[0], axis=0
+    )
     full_weight = lax.all_gather(rows_half, "pair", axis=1, tiled=True)
     rank_projection = jnp.dot(hidden_rows, adapter_down, preferred_element_type=jnp.float32).astype(
         jnp.bfloat16

time: 363 us -> 376 us (1.036)
  starting transfers between devices: 55.1 us -> 63.5 us
  local copies, waits for them, and re-layouts: 37.7 us -> 45.1 us
  blocking collectives: 30.3 us -> 23.9 us
    ppermute x0 -> x7, waiting for transfers between devices: none -> 65.9 us  [shards(): lax.ppermute(ring[-1], 'ctx', [(dev, (dev + 1) % 8) for dev in range(8)])]
    all_gather x1 -> x0, waiting for transfers between devices: 58.9 us -> none  [shards(): rows_half = lax.all_gather(own_half, 'ctx', axis=0, tiled=True)]
    psum x1, blocking collectives: 30.3 us -> 23.9 us  [shards(): own_diff, counts = lax.psum((part_diff, part_count), 'ctx')]
    ppermute x28, starting transfers between devices: 55 us -> 61 us  [shifted(): return lax.ppermute(block, axis, route)]
    unnamed x48 -> x59, local copies, waits for them, and re-layouts: 17.1 us -> 19.4 us
  transfers between devices with their start and end apart: 32 -> 38, of which waited for: 11 -> 17; matrix products, arithmetic and copies ran while one was open for 16% -> 16% of each run, Pallas kernels for 0% -> 0%
where the time goes in v1:
time: 376 us; the launch traced here: 375 us
  waiting for transfers between devices  190 us (51%)
  starting transfers between devices  63.5 us (17%)
  local copies, waits for them, and re-layouts  45.1 us (12%)
  matrix products  31.9 us (8%)
  blocking collectives  23.9 us (6%)
  between operations  14.8 us (4%)
  other arithmetic  5.23 us (1%)
    psum x1, waiting for transfers between devices, shards(): lax.psum((down_factor, up_factor), ('ctx', 'pair'))  73.1 us
    ppermute x7, waiting for transfers between devices, shards(): lax.ppermute(ring[-1], 'ctx', [(dev, (dev + 1) % 8) for dev in range(8)])  65.9 us
    ppermute x28, starting transfers between devices, shifted(): return lax.ppermute(block, axis, route)  61 us
    ppermute x28, waiting for transfers between devices, shifted(): return lax.ppermute(block, axis, route)  51.3 us
    psum x1, blocking collectives, shards(): own_diff, counts = lax.psum((part_diff, part_count), 'ctx')  23.9 us
    unnamed x59, local copies, waits for them, and re-layouts  19.4 us
    convert_element_type x7, local copies, waits for them, and re-layouts, shards(): key_parts[block_start:block_start + tok_rows].astype(jnp.bfloat16)  11.6 us
  transfers between devices with their start and end apart: 38, of which 17 were waited for; matrix products, arithmetic and copies ran while one was open for 16% of the time, Pallas kernels for 0%

profile of v1, /device:TPU:8, one launch (start us, length us, event | category | flops | bytes accessed | tf_op | source)
XLA Modules:
  0.0 374.8 jit_solution(16348364651502858130)
XLA Ops:
  9.9 9.2 %collective-permute-done.7 = bf16[336,512]{1,0:T(8,128)(2,1)S(1)} collective-permute-done((bf16[336,512]{1,0:T(8,128)(2,1)S(1)}, bf16[336,512]{1,0:T(8,128)(2,1)S(1)}, u32[]{:S(2)}, u32[]{:S(2)}) %collective-permute-start.7) | collective-permute-done | bytes 344096 | tf_op jit(solution)/shard_map/ppermute | solution.py:50
  19.7 9.2 %collective-permute-done.8 = bf16[336,512]{1,0:T(8,128)(2,1)S(1)} collective-permute-done((bf16[336,512]{1,0:T(8,128)(2,1)S(1)}, bf16[336,512]{1,0:T(8,128)(2,1)S(1)}, u32[]{:S(2)}, u32[]{:S(2)}) %collective-permute-start.8) | collective-permute-done | bytes 344096 | tf_op jit(solution)/shard_map/ppermute | solution.py:50
  28.9 8.9 %collective-permute-done.9 = bf16[336,512]{1,0:T(8,128)(2,1)S(1)} collective-permute-done((bf16[336,512]{1,0:T(8,128)(2,1)S(1)}, bf16[336,512]{1,0:T(8,128)(2,1)S(1)}, u32[]{:S(2)}, u32[]{:S(2)}) %collective-permute-start.9) | collective-permute-done | bytes 344096 | tf_op jit(solution)/shard_map/ppermute | solution.py:50
  37.8 9.5 %collective-permute-done.10 = bf16[336,512]{1,0:T(8,128)(2,1)S(1)} collective-permute-done((bf16[336,512]{1,0:T(8,128)(2,1)S(1)}, bf16[336,512]{1,0:T(8,128)(2,1)S(1)}, u32[]{:S(2)}, u32[]{:S(2)}) %collective-permute-start.10) | collective-permute-done | bytes 344096 | tf_op jit(solution)/shard_map/ppermute | solution.py:50
  47.4 9.4 %collective-permute-done.11 = bf16[336,512]{1,0:T(8,128)(2,1)S(1)} collective-permute-done((bf16[336,512]{1,0:T(8,128)(2,1)S(1)}, bf16[336,512]{1,0:T(8,128)(2,1)S(1)}, u32[]{:S(2)}, u32[]{:S(2)}) %collective-permute-start.11) | collective-permute-done | bytes 344096 | tf_op jit(solution)/shard_map/ppermute | solution.py:50
  56.8 9.7 %collective-permute-done.12 = bf16[336,512]{1,0:T(8,128)(2,1)S(1)} collective-permute-done((bf16[336,512]{1,0:T(8,128)(2,1)S(1)}, bf16[336,512]{1,0:T(8,128)(2,1)S(1)}, u32[]{:S(2)}, u32[]{:S(2)}) %collective-permute-start.12) | collective-permute-done | bytes 344096 | tf_op jit(solution)/shard_map/ppermute | solution.py:50
  66.7 10.0 %collective-permute-done.13 = bf16[336,512]{1,0:T(8,128)(2,1)} collective-permute-done((bf16[336,512]{1,0:T(8,128)(2,1)S(1)}, bf16[336,512]{1,0:T(8,128)(2,1)}, u32[]{:S(2)}, u32[]{:S(2)}) %collective-permute-start.13) | collective-permute-done | bytes 344096 | tf_op jit(solution)/shard_map/ppermute | solution.py:50
  79.2 2.2 constant_dynamic-slice_fusion
  83.5 9.4 %collective-permute-start.2 = (bf16[128,1024]{1,0:T(8,128)(2,1)}, bf16[128,1024]{1,0:T(8,128)(2,1)}, u32[]{:S(2)}, u32[]{:S(2)}) collective-permute-start(bf16[128,1024]{1,0:T(8,128)(2,1)} %bitcast.3), channel_id=1, source_target_pairs={{0,10},{2,12},{4,14},{1,11},{3,13},{5,15},{16,26},{18,28},{20,30},... | collective-permute-start | bytes 786440 | tf_op jit(solution)/shard_map/ppermute | solution.py:23
  92.9 2.0 collective-permute-start.3
  95.1 23.9 %all-reduce.1 = (f32[8]{0:T(128)S(1)}, f32[8]{0:T(128)S(1)}) all-reduce(f32[8]{0:T(128)S(1)} %get-tuple-element.21, f32[8]{0:T(128)S(1)} %get-tuple-element.22), channel_id=1, replica_groups=mesh['grp'=2,'ctx'=8,'pair'=2] {'ctx'}, use_global_device_ids=true, to_apply=%region_1.2 | all-reduce | flops 16 | bytes 128 | tf_op jit(solution)/shard_map/psum | solution.py:69
  122.1 2.7 collective-permute-start.4
  126.5 3.3 collective-permute-start.5
  135.7 3.8 %collective-permute-done.5 = bf16[128,1024]{1,0:T(8,128)(2,1)S(1)} collective-permute-done((bf16[128,1024]{1,0:T(8,128)(2,1)}, bf16[128,1024]{1,0:T(8,128)(2,1)S(1)}, u32[]{:S(2)}, u32[]{:S(2)}) %collective-permute-start.5) | collective-permute-done | bytes 262176 | tf_op jit(solution)/shard_map/ppermute | solution.py:23
  139.5 4.1 %collective-permute-done.6 = bf16[128,1024]{1,0:T(8,128)(2,1)S(1)} collective-permute-done((bf16[128,1024]{1,0:T(8,128)(2,1)}, bf16[128,1024]{1,0:T(8,128)(2,1)S(1)}, u32[]{:S(2)}, u32[]{:S(2)}) %collective-permute-start.6) | collective-permute-done | bytes 262176 | tf_op jit(solution)/shard_map/ppermute | solution.py:23
  144.6 4.9 %fusion.15 = bf16[128,1024]{0,1:T(8,128)(2,1)} fusion(f32[128,1024]{0,1:T(8,128)S(1)} %convolution_multiply_fusion.2, bf16[2688,1024]{1,0:T(8,128)(2,1)} %all-gather.2.cloned.1.call-done, bf16[1,128,2688]{2,1,0:T(8,128)(2,1)S(1)} %copy-done), kind=kOutput, calls=%fused_computation.28 | convolution fusion | flops 704905216 | bytes 6979584 | tf_op jit(solution)/shard_map/dot_general | solution.py:59
  152.4 2.3 collective-permute-start.24
  154.7 6.5 %collective-permute-start.25 = (bf16[128,1024]{0,1:T(8,128)(2,1)}, bf16[128,1024]{0,1:T(8,128)(2,1)}, u32[]{:S(2)}, u32[]{:S(2)}) collective-permute-start(bf16[128,1024]{0,1:T(8,128)(2,1)} %fusion.15), channel_id=1, source_target_pairs={{0,8},{2,10},{4,12},{6,14},{1,9},{3,11},{5,13},{7,15},{16,24},{18,... | collective-permute-start | bytes 786440 | tf_op jit(solution)/shard_map/ppermute | solution.py:23
  165.3 3.2 copy.60
  168.5 6.9 %fusion.36 = (f32[8,2,128]{2,1,0:T(2,128)S(1)}, f32[8,2,128,1024]{2,3,1,0:T(8,128)}) fusion(pred[128,1024]{0,1:T(8,128)(4,1)} %compare_and_fusion, bf16[1024,8,128,1]{0,2,3,1:T(8,128)(2,1)S(1)} %copy.60, bf16[128,8,2,128]{0,3,2,1:T(8,128)(2,1)S(1)} %bitcast.128), kind=kOutput, calls=%fused_computation.99 | convolution fusion | flops 547357696 | bytes 11149312 | tf_op jit(solution)/shard_map/sub | solution.py:104
  175.4 5.0 %fusion.37 = (bf16[1024,8,128]{0,2,1:T(8,128)(2,1)S(1)}, f32[1024,8,128]{0,2,1:T(8,128)S(1)}) fusion(bf16[128,8,2,128]{3,2,1,0:T(2,128)(2,1)} %reshape_squeeze.7, f32[128]{0:T(128)S(1)} %get-tuple-element.20, f32[8,2,128,1024]{2,3,1,0:T(8,128)} %get-tuple-element.42, f32[8,2,128]{2,1,0:T(2,128)S(1)} %get-tuple-element.41), kind=kOutput, calls=%fused_computation.100 | convolution fusion | flops 544210944 | bytes 15213056 | tf_op jit(solution)/shard_map/jgtl,tjgd->ljd/dot_general | solution.py:120
  181.0 3.0 collective-permute-start.27
  194.0 3.1 collective-permute-done.27
  206.2 3.4 collective-permute-start.16
  209.6 3.2 collective-permute-start.15
  212.8 3.4 fusion.38
  216.5 19.5 %collective-permute-done.17 = bf16[128,1024]{0,1:T(8,128)(2,1)S(1)} collective-permute-done((bf16[128,1024]{0,1:T(8,128)(2,1)S(1)}, bf16[128,1024]{0,1:T(8,128)(2,1)S(1)}, u32[]{:S(2)}, u32[]{:S(2)}) %collective-permute-start.17) | collective-permute-done | bytes 262176 | tf_op jit(solution)/shard_map/ppermute | solution.py:23
  238.7 2.0 copy.54
  265.4 5.3 %fusion.11 = bf16[1,128,2688]{2,1,0:T(8,128)(2,1)} fusion(f32[128,2688]{1,0:T(8,128)S(1)} %convolution_multiply_fusion, bf16[128,1024]{0,1:T(8,128)(2,1)S(1)} %fusion.27, bf16[2688,1024]{1,0:T(8,128)(2,1)} %all-gather.2.cloned.1.call-done), kind=kOutput, calls=%fused_computation.19 | convolution fusion | flops 705331200 | bytes 7831552 | tf_op jit(solution)/shard_map/tk,dk->td/dot_general | solution.py:138
  270.8 13.4 %collective-permute-done.31 = bf16[128,1024]{1,0:T(8,128)(2,1)} collective-permute-done((bf16[128,1024]{1,0:T(8,128)(2,1)}, bf16[128,1024]{1,0:T(8,128)(2,1)}, u32[]{:S(2)}, u32[]{:S(2)}) %collective-permute-start.31) | collective-permute-done | bytes 262176 | tf_op jit(solution)/shard_map/ppermute | solution.py:23
  284.2 5.1 %collective-permute-done.30 = bf16[128,1024]{1,0:T(8,128)(2,1)S(1)} collective-permute-done((bf16[128,1024]{1,0:T(8,128)(2,1)}, bf16[128,1024]{1,0:T(8,128)(2,1)S(1)}, u32[]{:S(2)}, u32[]{:S(2)}) %collective-permute-start.30) | collective-permute-done | bytes 262176 | tf_op jit(solution)/shard_map/ppermute | solution.py:23
  291.8 73.1 %all-reduce.4.cloned.1.call-done = (f32[2688,16]{0,1:T(8,128)}, f32[16,1024]{1,0:T(8,128)}) async-done(((f32[2688,16]{0,1:T(8,128)}, f32[16,1024]{1,0:T(8,128)}), (f32[2688,16]{0,1:T(8,128)}, f32[16,1024]{1,0:T(8,128)})) %all-reduce.4.cloned.1.call-update) | async-done | bytes 237584 | tf_op jit(solution)/shard_map/psum | solution.py:148
  (152 shorter events, 79.2 us)
Async XLA Ops:
  7.2 137.4 %all-gather.2.cloned.1.call-start = ((), (), s32[]{:S(2)}) async-start(), calls=%async_computation | async-start | bytes 8257536 | tf_op jit(solution)/shard_map/all_gather | solution.py:54
  8.4 10.8 %collective-permute-start.7 = (bf16[336,512]{1,0:T(8,128)(2,1)S(1)}, bf16[336,512]{1,0:T(8,128)(2,1)S(1)}, u32[]{:S(2)}, u32[]{:S(2)}) collective-permute-start(bf16[336,512]{1,0:T(8,128)(2,1)S(1)} %constant_dynamic-slice_fusion.1), channel_id=1, source_target_pairs={{0,2},{2,4},{4,6},{6,8},{8,10},{10,12},{12,14},{14,0},{1,3},{3,5},... | collective-permute-start | bytes 1032200 | tf_op jit(solution)/shard_map/ppermute | solution.py:50
  66.4 10.2 %collective-permute-start.13 = (bf16[336,512]{1,0:T(8,128)(2,1)S(1)}, bf16[336,512]{1,0:T(8,128)(2,1)}, u32[]{:S(2)}, u32[]{:S(2)}) collective-permute-start(bf16[336,512]{1,0:T(8,128)(2,1)S(1)} %collective-permute-done.12), channel_id=1, source_target_pairs={{0,2},{2,4},{4,6},{6,8},{8,10},{10,12},{12,14},{14,0},{1,3},{3,5},... | collective-permute-start | bytes 1032200 | tf_op jit(solution)/shard_map/ppermute | solution.py:50
  81.4 283.4 %all-reduce.4.cloned.1.call-start = ((), (), s32[]{:S(2)}) async-start(), calls=%async_computation.1 | async-start | bytes 475136 | tf_op jit(solution)/shard_map/psum | solution.py:148
  81.5 44.3 %collective-permute-start = (bf16[128,1024]{1,0:T(8,128)(2,1)}, bf16[128,1024]{1,0:T(8,128)(2,1)S(1)}, u32[]{:S(2)}, u32[]{:S(2)}) collective-permute-start(bf16[128,1024]{1,0:T(8,128)(2,1)} %bitcast.3), channel_id=1, source_target_pairs={{0,14},{1,15},{16,30},{17,31}} | collective-permute-start | bytes 786440 | tf_op jit(solution)/shard_map/ppermute | solution.py:23
  82.2 48.6 %collective-permute-start.1 = (bf16[128,1024]{1,0:T(8,128)(2,1)}, bf16[128,1024]{1,0:T(8,128)(2,1)}, u32[]{:S(2)}, u32[]{:S(2)}) collective-permute-start(bf16[128,1024]{1,0:T(8,128)(2,1)} %bitcast.3), channel_id=1, source_target_pairs={{0,12},{2,14},{1,13},{3,15},{16,28},{18,30},{17,29},{19,31}} | collective-permute-start | bytes 786440 | tf_op jit(solution)/shard_map/ppermute | solution.py:23
  83.5 50.2 %collective-permute-start.2 = (bf16[128,1024]{1,0:T(8,128)(2,1)}, bf16[128,1024]{1,0:T(8,128)(2,1)}, u32[]{:S(2)}, u32[]{:S(2)}) collective-permute-start(bf16[128,1024]{1,0:T(8,128)(2,1)} %bitcast.3), channel_id=1, source_target_pairs={{0,10},{2,12},{4,14},{1,11},{3,13},{5,15},{16,26},{18,28},{20,30},... | collective-permute-start | bytes 786440 | tf_op jit(solution)/shard_map/ppermute | solution.py:23
  92.9 41.7 %collective-permute-start.3 = (bf16[128,1024]{1,0:T(8,128)(2,1)}, bf16[128,1024]{1,0:T(8,128)(2,1)}, u32[]{:S(2)}, u32[]{:S(2)}) collective-permute-start(bf16[128,1024]{1,0:T(8,128)(2,1)} %bitcast.3), channel_id=1, source_target_pairs={{0,8},{2,10},{4,12},{6,14},{1,9},{3,11},{5,13},{7,15},{16,24},{18,... | collective-permute-start | bytes 786440 | tf_op jit(solution)/shard_map/ppermute | solution.py:23
  122.1 13.6 %collective-permute-start.4 = (bf16[128,1024]{1,0:T(8,128)(2,1)}, bf16[128,1024]{1,0:T(8,128)(2,1)S(1)}, u32[]{:S(2)}, u32[]{:S(2)}) collective-permute-start(bf16[128,1024]{1,0:T(8,128)(2,1)} %bitcast.3), channel_id=1, source_target_pairs={{0,6},{2,8},{4,10},{6,12},{8,14},{1,7},{3,9},{5,11},{7,13},{9,15},... | collective-permute-start | bytes 786440 | tf_op jit(solution)/shard_map/ppermute | solution.py:23
  126.5 13.0 %collective-permute-start.5 = (bf16[128,1024]{1,0:T(8,128)(2,1)}, bf16[128,1024]{1,0:T(8,128)(2,1)S(1)}, u32[]{:S(2)}, u32[]{:S(2)}) collective-permute-start(bf16[128,1024]{1,0:T(8,128)(2,1)} %bitcast.3), channel_id=1, source_target_pairs={{0,4},{2,6},{4,8},{6,10},{8,12},{10,14},{1,5},{3,7},{5,9},{7,11},{... | collective-permute-start | bytes 786440 | tf_op jit(solution)/shard_map/ppermute | solution.py:23
  130.8 12.8 %collective-permute-start.6 = (bf16[128,1024]{1,0:T(8,128)(2,1)}, bf16[128,1024]{1,0:T(8,128)(2,1)S(1)}, u32[]{:S(2)}, u32[]{:S(2)}) collective-permute-start(bf16[128,1024]{1,0:T(8,128)(2,1)} %bitcast.3), channel_id=1, source_target_pairs={{0,2},{2,4},{4,6},{6,8},{8,10},{10,12},{12,14},{1,3},{3,5},{5,7},{... | collective-permute-start | bytes 786440 | tf_op jit(solution)/shard_map/ppermute | solution.py:23
  149.5 31.5 %collective-permute-start.22 = (bf16[128,1024]{0,1:T(8,128)(2,1)}, bf16[128,1024]{0,1:T(8,128)(2,1)}, u32[]{:S(2)}, u32[]{:S(2)}) collective-permute-start(bf16[128,1024]{0,1:T(8,128)(2,1)} %fusion.15), channel_id=1, source_target_pairs={{0,14},{1,15},{16,30},{17,31}} | collective-permute-start | bytes 786440 | tf_op jit(solution)/shard_map/ppermute | solution.py:23
  151.0 34.0 %collective-permute-start.23 = (bf16[128,1024]{0,1:T(8,128)(2,1)}, bf16[128,1024]{0,1:T(8,128)(2,1)}, u32[]{:S(2)}, u32[]{:S(2)}) collective-permute-start(bf16[128,1024]{0,1:T(8,128)(2,1)} %fusion.15), channel_id=1, source_target_pairs={{0,12},{2,14},{1,13},{3,15},{16,28},{18,30},{17,29},{19,31}} | collective-permute-start | bytes 786440 | tf_op jit(solution)/shard_map/ppermute | solution.py:23
  152.4 35.6 %collective-permute-start.24 = (bf16[128,1024]{0,1:T(8,128)(2,1)}, bf16[128,1024]{0,1:T(8,128)(2,1)}, u32[]{:S(2)}, u32[]{:S(2)}) collective-permute-start(bf16[128,1024]{0,1:T(8,128)(2,1)} %fusion.15), channel_id=1, source_target_pairs={{0,10},{2,12},{4,14},{1,11},{3,13},{5,15},{16,26},{18,28},{20,30},... | collective-permute-start | bytes 786440 | tf_op jit(solution)/shard_map/ppermute | solution.py:23
  154.7 35.0 %collective-permute-start.25 = (bf16[128,1024]{0,1:T(8,128)(2,1)}, bf16[128,1024]{0,1:T(8,128)(2,1)}, u32[]{:S(2)}, u32[]{:S(2)}) collective-permute-start(bf16[128,1024]{0,1:T(8,128)(2,1)} %fusion.15), channel_id=1, source_target_pairs={{0,8},{2,10},{4,12},{6,14},{1,9},{3,11},{5,13},{7,15},{16,24},{18,... | collective-permute-start | bytes 786440 | tf_op jit(solution)/shard_map/ppermute | solution.py:23
  161.3 30.4 %collective-permute-start.26 = (bf16[128,1024]{0,1:T(8,128)(2,1)}, bf16[128,1024]{0,1:T(8,128)(2,1)}, u32[]{:S(2)}, u32[]{:S(2)}) collective-permute-start(bf16[128,1024]{0,1:T(8,128)(2,1)} %fusion.15), channel_id=1, source_target_pairs={{0,6},{2,8},{4,10},{6,12},{8,14},{1,7},{3,9},{5,11},{7,13},{9,15},... | collective-permute-start | bytes 786440 | tf_op jit(solution)/shard_map/ppermute | solution.py:23
  181.0 16.1 %collective-permute-start.27 = (bf16[128,1024]{0,1:T(8,128)(2,1)}, bf16[128,1024]{0,1:T(8,128)(2,1)S(1)}, u32[]{:S(2)}, u32[]{:S(2)}) collective-permute-start(bf16[128,1024]{0,1:T(8,128)(2,1)} %fusion.15), channel_id=1, source_target_pairs={{0,4},{2,6},{4,8},{6,10},{8,12},{10,14},{1,5},{3,7},{5,9},{7,11},{... | collective-permute-start | bytes 786440 | tf_op jit(solution)/shard_map/ppermute | solution.py:23
  185.0 13.5 %collective-permute-start.28 = (bf16[128,1024]{0,1:T(8,128)(2,1)}, bf16[128,1024]{0,1:T(8,128)(2,1)S(1)}, u32[]{:S(2)}, u32[]{:S(2)}) collective-permute-start(bf16[128,1024]{0,1:T(8,128)(2,1)} %fusion.15), channel_id=1, source_target_pairs={{0,2},{2,4},{4,6},{6,8},{8,10},{10,12},{12,14},{1,3},{3,5},{5,7},{... | collective-permute-start | bytes 786440 | tf_op jit(solution)/shard_map/ppermute | solution.py:23
  188.0 18.2 %collective-permute-start.21 = (bf16[128,1024]{0,1:T(8,128)(2,1)S(1)}, bf16[128,1024]{0,1:T(8,128)(2,1)S(1)}, u32[]{:S(2)}, u32[]{:S(2)}) collective-permute-start(bf16[128,1024]{0,1:T(8,128)(2,1)S(1)} %bitcast.143), channel_id=1, source_target_pairs={{14,0},{15,1},{30,16},{31,17}} | collective-permute-start | bytes 786440 | tf_op jit(solution)/shard_map/ppermute | solution.py:23
  189.7 19.9 %collective-permute-start.20 = (bf16[128,1024]{0,1:T(8,128)(2,1)S(1)}, bf16[128,1024]{0,1:T(8,128)(2,1)S(1)}, u32[]{:S(2)}, u32[]{:S(2)}) collective-permute-start(bf16[128,1024]{0,1:T(8,128)(2,1)S(1)} %bitcast.142), channel_id=1, source_target_pairs={{12,0},{14,2},{13,1},{15,3},{28,16},{30,18},{29,17},{31,19}} | collective-permute-start | bytes 786440 | tf_op jit(solution)/shard_map/ppermute | solution.py:23
  191.6 24.6 %collective-permute-start.19 = (bf16[128,1024]{0,1:T(8,128)(2,1)S(1)}, bf16[128,1024]{0,1:T(8,128)(2,1)S(1)}, u32[]{:S(2)}, u32[]{:S(2)}) collective-permute-start(bf16[128,1024]{0,1:T(8,128)(2,1)S(1)} %bitcast.141), channel_id=1, source_target_pairs={{10,0},{12,2},{14,4},{11,1},{13,3},{15,5},{26,16},{28,18},{30,20},... | collective-permute-start | bytes 786440 | tf_op jit(solution)/shard_map/ppermute | solution.py:23
  197.1 19.4 %collective-permute-start.18 = (bf16[128,1024]{0,1:T(8,128)(2,1)S(1)}, bf16[128,1024]{0,1:T(8,128)(2,1)S(1)}, u32[]{:S(2)}, u32[]{:S(2)}) collective-permute-start(bf16[128,1024]{0,1:T(8,128)(2,1)S(1)} %bitcast.140), channel_id=1, source_target_pairs={{8,0},{10,2},{12,4},{14,6},{9,1},{11,3},{13,5},{15,7},{24,16},{26,... | collective-permute-start | bytes 786440 | tf_op jit(solution)/shard_map/ppermute | solution.py:23
  198.5 37.6 %collective-permute-start.17 = (bf16[128,1024]{0,1:T(8,128)(2,1)S(1)}, bf16[128,1024]{0,1:T(8,128)(2,1)S(1)}, u32[]{:S(2)}, u32[]{:S(2)}) collective-permute-start(bf16[128,1024]{0,1:T(8,128)(2,1)S(1)} %bitcast.139), channel_id=1, source_target_pairs={{6,0},{8,2},{10,4},{12,6},{14,8},{7,1},{9,3},{11,5},{13,7},{15,9},... | collective-permute-start | bytes 786440 | tf_op jit(solution)/shard_map/ppermute | solution.py:23
  206.2 31.3 %collective-permute-start.16 = (bf16[128,1024]{0,1:T(8,128)(2,1)S(1)}, bf16[128,1024]{0,1:T(8,128)(2,1)S(1)}, u32[]{:S(2)}, u32[]{:S(2)}) collective-permute-start(bf16[128,1024]{0,1:T(8,128)(2,1)S(1)} %bitcast.138), channel_id=1, source_target_pairs={{4,0},{6,2},{8,4},{10,6},{12,8},{14,10},{5,1},{7,3},{9,5},{11,7},{... | collective-permute-start | bytes 786440 | tf_op jit(solution)/shard_map/ppermute | solution.py:23
  209.6 27.9 %collective-permute-start.15 = (bf16[128,1024]{0,1:T(8,128)(2,1)S(1)}, bf16[128,1024]{0,1:T(8,128)(2,1)S(1)}, u32[]{:S(2)}, u32[]{:S(2)}) collective-permute-start(bf16[128,1024]{0,1:T(8,128)(2,1)S(1)} %bitcast.137), channel_id=1, source_target_pairs={{2,0},{4,2},{6,4},{8,6},{10,8},{12,10},{14,12},{3,1},{5,3},{7,5},{... | collective-permute-start | bytes 786440 | tf_op jit(solution)/shard_map/ppermute | solution.py:23
  244.0 17.6 %collective-permute-start.35 = (bf16[128,1024]{1,0:T(8,128)(2,1)}, bf16[128,1024]{1,0:T(8,128)(2,1)S(1)}, u32[]{:S(2)}, u32[]{:S(2)}) collective-permute-start(bf16[128,1024]{1,0:T(8,128)(2,1)} %copy.53), channel_id=1, source_target_pairs={{14,0},{15,1},{30,16},{31,17}} | collective-permute-start | bytes 786440 | tf_op jit(solution)/shard_map/ppermute | solution.py:23
  246.5 17.0 %collective-permute-start.34 = (bf16[128,1024]{1,0:T(8,128)(2,1)}, bf16[128,1024]{1,0:T(8,128)(2,1)S(1)}, u32[]{:S(2)}, u32[]{:S(2)}) collective-permute-start(bf16[128,1024]{1,0:T(8,128)(2,1)} %copy.52), channel_id=1, source_target_pairs={{12,0},{14,2},{13,1},{15,3},{28,16},{30,18},{29,17},{31,19}} | collective-permute-start | bytes 786440 | tf_op jit(solution)/shard_map/ppermute | solution.py:23
  248.9 21.8 %collective-permute-start.33 = (bf16[128,1024]{1,0:T(8,128)(2,1)}, bf16[128,1024]{1,0:T(8,128)(2,1)S(1)}, u32[]{:S(2)}, u32[]{:S(2)}) collective-permute-start(bf16[128,1024]{1,0:T(8,128)(2,1)} %copy.51), channel_id=1, source_target_pairs={{10,0},{12,2},{14,4},{11,1},{13,3},{15,5},{26,16},{28,18},{30,20},... | collective-permute-start | bytes 786440 | tf_op jit(solution)/shard_map/ppermute | solution.py:23
  252.9 17.9 %collective-permute-start.32 = (bf16[128,1024]{1,0:T(8,128)(2,1)}, bf16[128,1024]{1,0:T(8,128)(2,1)S(1)}, u32[]{:S(2)}, u32[]{:S(2)}) collective-permute-start(bf16[128,1024]{1,0:T(8,128)(2,1)} %copy.50), channel_id=1, source_target_pairs={{8,0},{10,2},{12,4},{14,6},{9,1},{11,3},{13,5},{15,7},{24,16},{26,... | collective-permute-start | bytes 786440 | tf_op jit(solution)/shard_map/ppermute | solution.py:23
  256.0 28.2 %collective-permute-start.31 = (bf16[128,1024]{1,0:T(8,128)(2,1)}, bf16[128,1024]{1,0:T(8,128)(2,1)}, u32[]{:S(2)}, u32[]{:S(2)}) collective-permute-start(bf16[128,1024]{1,0:T(8,128)(2,1)} %copy.49), channel_id=1, source_target_pairs={{6,0},{8,2},{10,4},{12,6},{14,8},{7,1},{9,3},{11,5},{13,7},{15,9},... | collective-permute-start | bytes 786440 | tf_op jit(solution)/shard_map/ppermute | solution.py:23
  261.6 27.7 %collective-permute-start.30 = (bf16[128,1024]{1,0:T(8,128)(2,1)}, bf16[128,1024]{1,0:T(8,128)(2,1)S(1)}, u32[]{:S(2)}, u32[]{:S(2)}) collective-permute-start(bf16[128,1024]{1,0:T(8,128)(2,1)} %copy.48), channel_id=1, source_target_pairs={{4,0},{6,2},{8,4},{10,6},{12,8},{14,10},{5,1},{7,3},{9,5},{11,7},{... | collective-permute-start | bytes 786440 | tf_op jit(solution)/shard_map/ppermute | solution.py:23
  263.5 26.3 %collective-permute-start.29 = (bf16[128,1024]{1,0:T(8,128)(2,1)}, bf16[128,1024]{1,0:T(8,128)(2,1)S(1)}, u32[]{:S(2)}, u32[]{:S(2)}) collective-permute-start(bf16[128,1024]{1,0:T(8,128)(2,1)} %copy.46), channel_id=1, source_target_pairs={{2,0},{4,2},{6,4},{8,6},{10,8},{12,10},{14,12},{3,1},{5,3},{7,5},{... | collective-permute-start | bytes 786440 | tf_op jit(solution)/shard_map/ppermute | solution.py:23
  (19 other events, 510.0 us)
Sparse Core Ops, SparseCore 0:
  81.6 20.7 all-gather.1
  261.3 103.5 all-reduce.3
